TPU v7x, 32 devices: a whole 2x2x4 slice. The times are simulated.
32 devices in a mesh: tm: 16 (over z, x, core), doc: 2 (over y).
Axes of the slice: x: 2, y: 2, z: 4, core: 2. Of those that a mesh axis runs over, the one named last changes fastest.
Arguments:
- beta: float32 [16, 4096, 128], P('tm', 'doc'), may hold values from -6 to 260
- word_ids: int32 [16, 8, 128], P('tm', 'doc'), may hold values from 0 to 4095
- word_counts: int32 [16, 8, 128], P('tm', 'doc'), may hold values from 1 to 8
- block_slot: int32 [32], replicated, may hold values from 0 to 31, each once
- topic_prior: float32 [128], replicated, may hold values from 0.05 to 0.5
- drift_var: float32 [128], replicated, may hold values from 0.0005 to 0.05
- obs_precision: float32 [16, 128], replicated, may hold values from 0.01 to 4
Outputs:
- smoothed_means: float32 [16, 4096, 128], P('tm', 'doc')
- doc_topics: float32 [16, 8, 128], P('tm', 'doc')
Inputs may be any that keep to these rules, and one draw needn't show every extreme that they name: `block_slot`: each block has its own position.
All inputs are finite; a program needn't handle non-finite values.
Results may differ from a plain program's by a relative error of at most 0.0012.
The roundings to bfloat16 on the way count: a program that leaves them out, or rounds other values in their place, can miss the bound.
Values may be sent and summed in bfloat16 or wider, within the bound.
No kernel may reach another device: no remote copies, remote signals or barrier semaphores. Data moves between devices by JAX's collectives and lax.ppermute only.
A program may use at most 192 MiB of HBM per device.

v0:
```python
import jax
import jax.numpy as jnp
from jax import lax
from jax.sharding import PartitionSpec as P

K = 128
BLOCK = 128
EITERS = 4
init_variance = 4.0


def variance_tables(obs_precision, drift_var):

    def forward_step(prior_var, precision):
        denominator = 1.0 + prior_var * precision
        gain_now = prior_var * precision / denominator
        filt_var = prior_var / denominator
        return (filt_var + drift_var, (gain_now, filt_var))

    start_var = jnp.full(drift_var.shape, init_variance, dtype=jnp.float32)
    last_var, (gains, filt_vars) = lax.scan(forward_step, start_var, obs_precision)

    def backward_step(info_next, precision):
        merged = info_next + precision
        shrink = 1.0 / (1.0 + drift_var * merged)
        info_now = merged * shrink
        return (info_now, (shrink, info_now))

    zero_info = jnp.zeros(drift_var.shape, dtype=jnp.float32)
    last_info, (shrinks, infos) = lax.scan(
        backward_step, zero_info, obs_precision[1:], reverse=True
    )
    shrinks = jnp.concatenate([shrinks, jnp.ones_like(zero_info)[None]], axis=0)
    infos = jnp.concatenate([infos, zero_info[None]], axis=0)
    return (gains, filt_vars, shrinks, infos)


def e_step(looked, word_counts, topic_prior):
    counts_float = word_counts.astype(jnp.float32)
    doc_topics = topic_prior + jnp.sum(counts_float, axis=-1, keepdims=True) / K
    scores = looked.astype(jnp.float32)
    for sweep in range(EITERS):
        resp = jax.nn.softmax(lax.digamma(doc_topics)[..., None, :] + scores, axis=-1)
        doc_topics = topic_prior + jnp.sum(counts_float[..., None] * resp, axis=-2)
    weighted = (counts_float[..., None] * resp).astype(jnp.bfloat16)
    return (doc_topics, weighted)


def body(beta, word_ids, word_counts, block_slot, topic_prior, drift_var, obs_precision):
    local_beta = beta[0]
    own_words = local_beta.shape[0]
    topics = local_beta.shape[1]
    doc_devices = lax.axis_size("doc")
    doc_place = lax.axis_index("doc")
    local_peak = jnp.max(local_beta, axis=0)
    local_total = jnp.sum(jnp.exp(local_beta - local_peak), axis=0)
    slot_ids = word_ids[0]
    local_docs = slot_ids.shape[0]
    slot_width = slot_ids.shape[1]
    columns = jnp.take(block_slot, slot_ids // BLOCK) * BLOCK + slot_ids % BLOCK
    all_columns = lax.all_gather(columns, "doc", axis=0, tiled=True)
    all_counts = lax.all_gather(word_counts[0], "doc", axis=0, tiled=True)
    peaks = lax.all_gather(local_peak, "doc")
    totals = lax.all_gather(local_total, "doc")
    peak_value = jnp.max(peaks, axis=0)
    total_value = jnp.sum(totals * jnp.exp(peaks - peak_value), axis=0)
    normalizer = peak_value + jnp.log(total_value)
    flat_columns = all_columns.reshape(-1)
    local_columns = flat_columns - doc_place * own_words
    inside = (local_columns >= 0) & (local_columns < own_words)
    picked = jnp.take(local_beta, jnp.clip(local_columns, 0, own_words - 1), axis=0)
    partial = jnp.where(
        inside[:, None], (picked - normalizer).astype(jnp.bfloat16), jnp.zeros((), jnp.bfloat16)
    )
    looked = lax.psum(partial, "doc").reshape(local_docs * doc_devices, slot_width, topics)
    doc_topics_all, weighted = e_step(looked, all_counts, topic_prior)
    doc_topics = lax.dynamic_slice_in_dim(doc_topics_all, doc_place * local_docs, local_docs, 0)
    flat_weighted = weighted.reshape(-1, topics)
    row_words = lax.iota(jnp.int32, own_words)
    marks = (row_words[:, None] == local_columns[None, :]).astype(jnp.bfloat16)
    counts = jnp.dot(marks, flat_weighted, preferred_element_type=jnp.float32)
    pseudo = local_beta + jnp.log1p(counts)
    gains, filt_vars, shrinks, infos = variance_tables(obs_precision, drift_var)
    years_total = obs_precision.shape[0]
    pulls = filt_vars / (filt_vars + drift_var)
    pulls = pulls.at[-1].set(0.0)
    years = lax.axis_size("tm")
    chunk = own_words // years
    by_year = lax.all_to_all(
        pseudo.reshape(years, chunk, topics), "tm", split_axis=0, concat_axis=0, tiled=True
    )

    def filter_step(mean_prev, inputs):
        gain_now, pseudo_now = inputs
        mean_now = (1.0 - gain_now) * mean_prev + gain_now * pseudo_now
        return (mean_now, mean_now)

    zero_mean = jnp.zeros((chunk, topics), dtype=jnp.float32)
    last_mean, filtered = lax.scan(
        filter_step, zero_mean, (gains[:, None, :], by_year), unroll=True
    )

    def smooth_step(mean_next, inputs):
        pull_now, filt_now = inputs
        mean_now = pull_now * mean_next + (1.0 - pull_now) * filt_now
        return (mean_now, mean_now)

    first_mean, smoothed = lax.scan(
        smooth_step, zero_mean, (pulls[:, None, :], filtered), reverse=True, unroll=True
    )
    back = lax.all_to_all(smoothed, "tm", split_axis=0, concat_axis=0, tiled=True)
    return (back.reshape(own_words, topics)[None], doc_topics[None])


def solution(mesh):
    in_specs = (
        P("tm", "doc", None),
        P("tm", "doc", None),
        P("tm", "doc", None),
        P(),
        P(),
        P(),
        P(),
    )
    out_specs = (P("tm", "doc", None), P("tm", "doc", None))
    return jax.shard_map(body, mesh=mesh, in_specs=in_specs, out_specs=out_specs, check_vma=False)
```

profile of v0, /device:TPU:9, one launch (start us, length us, event | category | flops | bytes accessed | tf_op | source)
XLA Modules:
  0.0 144.6 jit_solution(16217126004983186146)
XLA Ops:
  7.2 1.6 %reduce_max.54 = f32[128]{0:T(128)S(1)} reduce(f32[1,2048,128]{2,1,0:T(8,128)} %param.11, f32[]{:T(128)} %constant.154.clone.1), dimensions={0,1}, to_apply=%region_3.4 | reduce | flops 262016 | bytes 1049092 | tf_op jit(solution)/shard_map/reduce_max | solution.py:55
  8.8 0.3 exponential_reduce_fusion
  9.1 3.1 %all-gather.5 = f32[2,1,128]{2,1,0:T(1,128)S(1)} all-gather(f32[1,1,128]{2,1,0:T(1,128)S(1)} %bitcast.281), channel_id=4, replica_groups=mesh['tm'=16,'doc'=2] {'doc'}, dimensions={0}, use_global_device_ids=true | all-gather | bytes 1536 | tf_op jit(solution)/shard_map/all_gather | solution.py:64
  12.2 3.1 %all-gather.4 = f32[2,1,128]{2,1,0:T(1,128)S(1)} all-gather(f32[1,1,128]{2,1,0:T(1,128)S(1)} %bitcast.278), channel_id=3, replica_groups=mesh['tm'=16,'doc'=2] {'doc'}, dimensions={0}, use_global_device_ids=true | all-gather | bytes 1536 | tf_op jit(solution)/shard_map/all_gather | solution.py:63
  15.4 3.3 %gather_fusion = s32[512]{0:T(512)S(1)} fusion(s32[32]{0:T(128)S(1)} %copy-done, s32[1024]{0:T(1024)S(1)} %pad_clamp_fusion), kind=kCustom, calls=%fused_computation | custom fusion | bytes 6144 | tf_op jit(solution)/shard_map/jit(_take)/gather | solution.py:60
  18.8 3.2 %all-gather.3 = s32[2,4,128]{2,1,0:T(4,128)S(1)} all-gather(s32[1,4,128]{2,1,0:T(4,128)S(1)} %fusion.120), channel_id=1, replica_groups=mesh['tm'=16,'doc'=2] {'doc'}, dimensions={0}, use_global_device_ids=true | all-gather | bytes 6144 | tf_op jit(solution)/shard_map/all_gather | solution.py:61
  22.0 2.8 %gather_fusion.1 = f32[1024,128]{1,0:T(8,128)S(1)} fusion(f32[2048,128]{1,0:T(8,128)S(1)} %bitcast.257, s32[1024]{0:T(1024)S(1)} %broadcast_clamp_fusion), kind=kCustom, calls=%fused_computation.1 | custom fusion | bytes 1052672 | tf_op jit(solution)/shard_map/jit(_take)/gather | solution.py:71
  24.9 1.0 fusion.24
  25.9 3.2 %all-gather = s32[1,8,128]{2,0,1:T(1,128)S(1)} all-gather(s32[1,4,128]{2,0,1:T(1,128)S(1)} %bitcast.279), channel_id=2, replica_groups=mesh['tm'=16,'doc'=2] {'doc'}, dimensions={1}, use_global_device_ids=true | all-gather | bytes 6144 | tf_op jit(solution)/shard_map/all_gather | solution.py:62
  29.2 0.1 convert_reduce_fusion
  29.5 24.0 %all-reduce.2.cloned.1.call-done = bf16[1024,128]{1,0:T(8,128)(2,1)} async-done(((bf16[1024,128]{1,0:T(8,128)(2,1)}), bf16[1024,128]{1,0:T(8,128)(2,1)}) %all-reduce.2.cloned.1.call-update) | async-done | bytes 262160 | tf_op jit(solution)/shard_map/psum | solution.py:75
  53.5 1.2 fusion.6
  54.7 1.3 fusion.23
  56.1 1.4 multiply_reduce_fusion.3
  57.5 1.2 fusion.8
  58.7 0.4 fusion.21
  59.1 0.5 multiply_reduce_fusion.2
  59.7 0.2 fusion.10
  59.9 0.4 fusion.19
  60.3 0.5 multiply_reduce_fusion.1
  60.8 0.2 fusion.12
  61.1 0.4 fusion.15
  61.5 0.5 fusion.17
  61.9 2.8 %fusion.4 = f32[2048,128]{1,0:T(8,128)} fusion(bf16[1024,128]{1,0:T(8,128)(2,1)S(1)} %fusion.17, s32[1024]{0:T(1024)S(1)} %bitcast.274, f32[1,2048,128]{2,1,0:T(8,128)S(1)} %copy-done.2), kind=kOutput, calls=%fused_computation.11 | convolution fusion | flops 539230208 | bytes 2363392 | tf_op jit(solution)/shard_map/dot_general | solution.py:81
  64.7 7.0 %all-to-all-start = ((f32[16,128,128]{2,1,0:T(8,128)}), f32[16,128,128]{2,1,0:T(8,128)S(1)}, u32[]{:S(2)}, u32[]{:S(2)}) async-start(f32[16,128,128]{2,1,0:T(8,128)} %bitcast.59), calls=%async_computation | async-start | bytes 2097152 | tf_op jit(solution)/shard_map/all_to_all | solution.py:89
  71.7 12.5 %while.16 = (s32[]{:T(128)}, f32[128]{0:T(128)S(1)}, f32[16,128]{1,0:T(8,128)S(1)}, f32[16,128]{1,0:T(8,128)S(1)}, f32[16,128]{1,0:T(8,128)}, /*index=5*/f32[128]{0:T(128)S(1)}, s32[]{:T(128)}, s32[]{:T(128)}) while((s32[]{:T(128)}, f32[128]{0:T(128)S(1)}, f32[16,128]{1,0:T(8,128)S(1)}, f32[16,128]{1,0:T(8,128)S(1)}, ...), condition=%wide.region_1.0_spmd.clone, body=%wide.region_0.0_spmd.clone.sunk | while | flops 771 | bytes 5235 | solution.py:21
  71.7 0.7 fusion.137
  72.5 0.7 fusion.137
  73.3 0.7 fusion.137
  74.1 0.7 fusion.137
  74.8 0.7 fusion.137
  75.6 0.7 fusion.137
  76.4 0.7 fusion.137
  77.2 0.7 fusion.137
  78.0 0.7 fusion.137
  78.8 0.7 fusion.137
  79.5 0.7 fusion.137
  80.3 0.7 fusion.137
  81.1 0.7 fusion.137
  81.9 0.7 fusion.137
  82.7 0.7 fusion.137
  83.5 0.7 fusion.137
  84.3 12.3 %all-to-all-done = f32[16,128,128]{2,1,0:T(8,128)S(1)} async-done(((f32[16,128,128]{2,1,0:T(8,128)}), f32[16,128,128]{2,1,0:T(8,128)S(1)}, u32[]{:S(2)}, u32[]{:S(2)}) %all-to-all-start) | async-done | bytes 1048608 | tf_op jit(solution)/shard_map/all_to_all | solution.py:89
  96.6 0.9 add_dynamic-update-slice_fusion
  97.6 0.6 constant_dynamic-update-slice_fusion.13
  98.2 0.6 constant_dynamic-update-slice_fusion.12
  98.8 0.6 constant_dynamic-update-slice_fusion.11
  99.5 0.6 constant_dynamic-update-slice_fusion.10
  100.1 0.6 constant_dynamic-update-slice_fusion.9
  100.7 0.6 constant_dynamic-update-slice_fusion.8
  101.4 0.6 constant_dynamic-update-slice_fusion.7
  102.0 0.6 constant_dynamic-update-slice_fusion.6
  102.6 0.6 constant_dynamic-update-slice_fusion.5
  103.3 0.6 constant_dynamic-update-slice_fusion.4
  103.9 0.6 constant_dynamic-update-slice_fusion.3
  104.6 0.6 constant_dynamic-update-slice_fusion.2
  105.2 0.6 constant_dynamic-update-slice_fusion.1
  105.8 0.6 constant_dynamic-update-slice_fusion
  106.5 0.6 fusion.41
  107.1 4.8 %all-to-all-start.1 = ((f32[16,128,128]{2,1,0:T(8,128)}), f32[16,128,128]{2,1,0:T(8,128)S(1)}, u32[]{:S(2)}, u32[]{:S(2)}) async-start(f32[16,128,128]{2,1,0:T(8,128)} %fusion.41), calls=%async_computation.1 | async-start | bytes 2097152 | tf_op jit(solution)/shard_map/all_to_all | solution.py:111
  111.9 0.5 multiply_reduce_fusion
  112.4 0.6 dynamic-slice_bitcast_fusion
  113.0 23.8 %all-to-all-done.1 = f32[16,128,128]{2,1,0:T(8,128)S(1)} async-done(((f32[16,128,128]{2,1,0:T(8,128)}), f32[16,128,128]{2,1,0:T(8,128)S(1)}, u32[]{:S(2)}, u32[]{:S(2)}) %all-to-all-start.1) | async-done | bytes 1048608 | tf_op jit(solution)/shard_map/all_to_all | solution.py:111
  136.8 1.0 copy.43
  (73 shorter events, 1.5 us)
Async XLA Ops:
  7.2 8.2 %copy-start = (s32[32]{0:T(128)S(1)}, s32[32]{0:T(128)}, u32[]{:S(2)}) copy-start(s32[32]{0:T(128)} %param.14) | copy-start | bytes 388
  7.2 1.7 %copy-start.2 = (f32[1,2048,128]{2,1,0:T(8,128)S(1)}, f32[1,2048,128]{2,1,0:T(8,128)}, u32[]{:S(2)}) copy-start(f32[1,2048,128]{2,1,0:T(8,128)} %param.11) | copy-start | bytes 3145732
  7.2 46.3 %all-reduce.2.cloned.1.call-start = ((), (), s32[]{:S(2)}) async-start(), calls=%async_computation.2 | async-start | bytes 524288 | tf_op jit(solution)/shard_map/psum | solution.py:75
  7.2 8.1 %copy-start.5 = (s32[1,4,128]{2,1,0:T(4,128)S(1)}, s32[1,4,128]{2,1,0:T(4,128)}, u32[]{:S(2)}) copy-start(s32[1,4,128]{2,1,0:T(4,128)} %param.12) | copy-start | bytes 6148
  24.8 1.1 copy-start.6
  24.8 4.5 %copy-start.4 = (f32[128]{0:T(128)S(1)}, f32[128]{0:T(128)}, u32[]{:S(2)}) copy-start(f32[128]{0:T(128)} %param.15) | copy-start | bytes 1540
  53.5 5.2 %copy-start.1 = (bf16[1024,128]{1,0:T(8,128)(2,1)S(1)}, bf16[1024,128]{1,0:T(8,128)(2,1)}, u32[]{:S(2)}) copy-start(bf16[1024,128]{1,0:T(8,128)(2,1)} %all-reduce.2.cloned.1.call-done) | copy-start | bytes 786436
  64.7 7.0 %copy-start.3 = (f32[128]{0:T(128)S(1)}, f32[128]{0:T(128)}, u32[]{:S(2)}) copy-start(f32[128]{0:T(128)} %param.16) | copy-start | bytes 1540
  64.7 31.9 %all-to-all-start = ((f32[16,128,128]{2,1,0:T(8,128)}), f32[16,128,128]{2,1,0:T(8,128)S(1)}, u32[]{:S(2)}, u32[]{:S(2)}) async-start(f32[16,128,128]{2,1,0:T(8,128)} %bitcast.59), calls=%async_computation | async-start | bytes 2097152 | tf_op jit(solution)/shard_map/all_to_all | solution.py:89
  107.1 29.7 %all-to-all-start.1 = ((f32[16,128,128]{2,1,0:T(8,128)}), f32[16,128,128]{2,1,0:T(8,128)S(1)}, u32[]{:S(2)}, u32[]{:S(2)}) async-start(f32[16,128,128]{2,1,0:T(8,128)} %fusion.41), calls=%async_computation.1 | async-start | bytes 2097152 | tf_op jit(solution)/shard_map/all_to_all | solution.py:111
Sparse Core Ops, SparseCore 0:
  26.0 27.4 all-reduce.1
where the time goes:
time: 146 us; the launch traced here: 145 us
  waiting for transfers between devices  60.2 us (41%)
  other arithmetic  29.6 us (20%)
  between operations  14.3 us (10%)
  local copies, waits for them, and re-layouts  13.1 us (9%)
  blocking collectives  12.6 us (9%)
  starting transfers between devices  11.8 us (8%)
  matrix products  2.76 us (2%)
    psum x1, waiting for transfers between devices, body(): lax.psum(partial, 'doc')  24 us
    all_to_all x1, waiting for transfers between devices, body(): lax.all_to_all(smoothed, 'tm', split_axis=0, concat_axis=0, tiled=True)  23.8 us
    all_to_all x1, waiting for transfers between devices, body(): lax.all_to_all(pseudo.reshape(years, chunk, topics), 'tm', split_axis=0,...  12.3 us
    add x16, other arithmetic, forward_step(): return (filt_var + drift_var, (gain_now, filt_var))  11.4 us
    all_to_all x1, starting transfers between devices, body(): lax.all_to_all(pseudo.reshape(years, chunk, topics), 'tm', split_axis=0,...  6.99 us
    unnamed x22, local copies, waits for them, and re-layouts  5.44 us
    unnamed x10, other arithmetic  5.43 us
    all_to_all x1, starting transfers between devices, body(): lax.all_to_all(smoothed, 'tm', split_axis=0, concat_axis=0, tiled=True)  4.76 us
  transfers between devices with their start and end apart: 3, of which 3 were waited for; matrix products, arithmetic and copies ran while one was open for 9% of the time, Pallas kernels for 0%

commit v1 on v0

--- a/solution.py
+++ b/solution.py
@@ -7,6 +7,18 @@
 BLOCK = 128
 EITERS = 4
 init_variance = 4.0
+
+
+def gather_by_bits(x, axis, dim):
+    ways, here, lap = (lax.axis_size(axis), lax.axis_index(axis), x.shape[dim])
+    line, have = (x, 1)
+    while have < ways:
+        line = jnp.concatenate(
+            [line, lax.ppermute(line, axis, [(d, (d - have) % ways) for d in range(ways)])],
+            axis=dim,
+        )
+        have = 2 * have
+    return jnp.roll(line, here * lap, axis=dim)
 
 
 def variance_tables(obs_precision, drift_var):
@@ -59,7 +71,7 @@
     slot_width = slot_ids.shape[1]
     columns = jnp.take(block_slot, slot_ids // BLOCK) * BLOCK + slot_ids % BLOCK
     all_columns = lax.all_gather(columns, "doc", axis=0, tiled=True)
-    all_counts = lax.all_gather(word_counts[0], "doc", axis=0, tiled=True)
+    all_counts = gather_by_bits(word_counts[0], "doc", 0)
     peaks = lax.all_gather(local_peak, "doc")
     totals = lax.all_gather(local_total, "doc")
     peak_value = jnp.max(peaks, axis=0)

time: 146 us -> 146 us (level)
  blocking collectives: 12.6 us -> 9.36 us
  waiting for transfers between devices: 60.2 us -> 62.7 us
    all_gather x1 -> x0, blocking collectives: 3.21 us -> none  [body(): all_counts = lax.all_gather(word_counts[0], 'doc', axis=0, tiled=True)]
    psum x1, waiting for transfers between devices: 24 us -> 26.5 us  [body(): lax.psum(partial, 'doc')]
  transfers between devices with their start and end apart: 3 -> 4, of which waited for: 3 -> 3; matrix products, arithmetic and copies ran while one was open for 9% -> 16% of each run, Pallas kernels for 0% -> 0%
where the time goes in v1:
time: 146 us; the launch traced here: 145 us
  waiting for transfers between devices  62.7 us (43%)
  other arithmetic  29.5 us (20%)
  between operations  14.4 us (10%)
  local copies, waits for them, and re-layouts  13.1 us (9%)
  starting transfers between devices  13.1 us (9%)
  blocking collectives  9.36 us (6%)
  matrix products  2.76 us (2%)
    psum x1, waiting for transfers between devices, body(): lax.psum(partial, 'doc')  26.5 us
    all_to_all x1, waiting for transfers between devices, body(): lax.all_to_all(smoothed, 'tm', split_axis=0, concat_axis=0, tiled=True)  23.8 us
    all_to_all x1, waiting for transfers between devices, body(): lax.all_to_all(pseudo.reshape(years, chunk, topics), 'tm', split_axis=0,...  12.3 us
    add x16, other arithmetic, forward_step(): return (filt_var + drift_var, (gain_now, filt_var))  11.4 us
    all_to_all x1, starting transfers between devices, body(): lax.all_to_all(pseudo.reshape(years, chunk, topics), 'tm', split_axis=0,...  6.99 us
    unnamed x22, local copies, waits for them, and re-layouts  5.44 us
    unnamed x10, other arithmetic  5.43 us
    all_to_all x1, starting transfers between devices, body(): lax.all_to_all(smoothed, 'tm', split_axis=0, concat_axis=0, tiled=True)  4.76 us
  transfers between devices with their start and end apart: 4, of which 3 were waited for; matrix products, arithmetic and copies ran while one was open for 16% of the time, Pallas kernels for 0%

profile of v1, /device:TPU:9, one launch (start us, length us, event | category | flops | bytes accessed | tf_op | source)
XLA Modules:
  0.0 145.2 jit_solution(3726495791568473969)
XLA Ops:
  7.2 1.3 collective-permute-start
  8.5 1.5 %reduce_max.54 = f32[128]{0:T(128)S(1)} reduce(f32[1,2048,128]{2,1,0:T(8,128)} %param.11, f32[]{:T(128)} %constant.175.clone.1), dimensions={0,1}, to_apply=%region_3.4 | reduce | flops 262016 | bytes 1049092 | tf_op jit(solution)/shard_map/reduce_max | solution.py:67
  10.1 0.3 exponential_reduce_fusion
  10.4 3.1 %all-gather.4 = f32[2,1,128]{2,1,0:T(1,128)S(1)} all-gather(f32[1,1,128]{2,1,0:T(1,128)S(1)} %bitcast.277), channel_id=3, replica_groups=mesh['tm'=16,'doc'=2] {'doc'}, dimensions={0}, use_global_device_ids=true | all-gather | bytes 1536 | tf_op jit(solution)/shard_map/all_gather | solution.py:76
  13.4 3.1 %all-gather.3 = f32[2,1,128]{2,1,0:T(1,128)S(1)} all-gather(f32[1,1,128]{2,1,0:T(1,128)S(1)} %bitcast.273), channel_id=2, replica_groups=mesh['tm'=16,'doc'=2] {'doc'}, dimensions={0}, use_global_device_ids=true | all-gather | bytes 1536 | tf_op jit(solution)/shard_map/all_gather | solution.py:75
  16.6 3.3 %gather_fusion = s32[512]{0:T(512)S(1)} fusion(s32[32]{0:T(128)S(1)} %copy-done, s32[1024]{0:T(1024)S(1)} %pad_clamp_fusion), kind=kCustom, calls=%fused_computation | custom fusion | bytes 6144 | tf_op jit(solution)/shard_map/jit(_take)/gather | solution.py:72
  20.0 3.2 %all-gather.2 = s32[2,4,128]{2,1,0:T(4,128)S(1)} all-gather(s32[1,4,128]{2,1,0:T(4,128)S(1)} %fusion.124), channel_id=1, replica_groups=mesh['tm'=16,'doc'=2] {'doc'}, dimensions={0}, use_global_device_ids=true | all-gather | bytes 6144 | tf_op jit(solution)/shard_map/all_gather | solution.py:73
  23.2 2.8 %gather_fusion.1 = f32[1024,128]{1,0:T(8,128)S(1)} fusion(f32[2048,128]{1,0:T(8,128)S(1)} %bitcast.256, s32[1024]{0:T(1024)S(1)} %broadcast_clamp_fusion), kind=kCustom, calls=%fused_computation.1 | custom fusion | bytes 1052672 | tf_op jit(solution)/shard_map/jit(_take)/gather | solution.py:83
  26.1 1.0 fusion.24
  27.2 0.1 fusion.139
  27.5 26.5 %all-reduce.2.cloned.1.call-done = bf16[1024,128]{1,0:T(8,128)(2,1)} async-done(((bf16[1024,128]{1,0:T(8,128)(2,1)}), bf16[1024,128]{1,0:T(8,128)(2,1)}) %all-reduce.2.cloned.1.call-update) | async-done | bytes 262160 | tf_op jit(solution)/shard_map/psum | solution.py:87
  54.1 1.2 fusion.6
  55.3 1.3 fusion.23
  56.6 1.4 multiply_reduce_fusion.3
  58.1 1.2 fusion.8
  59.3 0.4 fusion.21
  59.7 0.5 multiply_reduce_fusion.2
  60.2 0.2 fusion.10
  60.5 0.4 fusion.19
  60.8 0.5 multiply_reduce_fusion.1
  61.4 0.2 fusion.12
  61.6 0.4 fusion.15
  62.0 0.5 fusion.17
  62.5 2.8 %fusion.4 = f32[2048,128]{1,0:T(8,128)} fusion(bf16[1024,128]{1,0:T(8,128)(2,1)S(1)} %fusion.17, s32[1024]{0:T(1024)S(1)} %bitcast.269, f32[1,2048,128]{2,1,0:T(8,128)S(1)} %copy-done.2), kind=kOutput, calls=%fused_computation.11 | convolution fusion | flops 539230208 | bytes 2363392 | tf_op jit(solution)/shard_map/dot_general | solution.py:93
  65.3 7.0 %all-to-all-start = ((f32[16,128,128]{2,1,0:T(8,128)}), f32[16,128,128]{2,1,0:T(8,128)S(1)}, u32[]{:S(2)}, u32[]{:S(2)}) async-start(f32[16,128,128]{2,1,0:T(8,128)} %bitcast.58), calls=%async_computation | async-start | bytes 2097152 | tf_op jit(solution)/shard_map/all_to_all | solution.py:101
  72.3 12.5 %while.16 = (s32[]{:T(128)}, f32[128]{0:T(128)S(1)}, f32[16,128]{1,0:T(8,128)S(1)}, f32[16,128]{1,0:T(8,128)S(1)}, f32[16,128]{1,0:T(8,128)}, /*index=5*/f32[128]{0:T(128)S(1)}, s32[]{:T(128)}, s32[]{:T(128)}) while((s32[]{:T(128)}, f32[128]{0:T(128)S(1)}, f32[16,128]{1,0:T(8,128)S(1)}, f32[16,128]{1,0:T(8,128)S(1)}, ...), condition=%wide.region_1.0_spmd.clone, body=%wide.region_0.0_spmd.clone.sunk | while | flops 771 | bytes 5235 | solution.py:33
  72.3 0.7 fusion.143
  73.0 0.7 fusion.143
  73.8 0.7 fusion.143
  74.6 0.7 fusion.143
  75.4 0.7 fusion.143
  76.2 0.7 fusion.143
  77.0 0.7 fusion.143
  77.7 0.7 fusion.143
  78.5 0.7 fusion.143
  79.3 0.7 fusion.143
  80.1 0.7 fusion.143
  80.9 0.7 fusion.143
  81.7 0.7 fusion.143
  82.4 0.7 fusion.143
  83.2 0.7 fusion.143
  84.0 0.7 fusion.143
  84.9 12.3 %all-to-all-done = f32[16,128,128]{2,1,0:T(8,128)S(1)} async-done(((f32[16,128,128]{2,1,0:T(8,128)}), f32[16,128,128]{2,1,0:T(8,128)S(1)}, u32[]{:S(2)}, u32[]{:S(2)}) %all-to-all-start) | async-done | bytes 1048608 | tf_op jit(solution)/shard_map/all_to_all | solution.py:101
  97.2 0.9 add_dynamic-update-slice_fusion
  98.1 0.6 constant_dynamic-update-slice_fusion.13
  98.7 0.6 constant_dynamic-update-slice_fusion.12
  99.4 0.6 constant_dynamic-update-slice_fusion.11
  100.0 0.6 constant_dynamic-update-slice_fusion.10
  100.7 0.6 constant_dynamic-update-slice_fusion.9
  101.3 0.6 constant_dynamic-update-slice_fusion.8
  101.9 0.6 constant_dynamic-update-slice_fusion.7
  102.6 0.6 constant_dynamic-update-slice_fusion.6
  103.2 0.6 constant_dynamic-update-slice_fusion.5
  103.8 0.6 constant_dynamic-update-slice_fusion.4
  104.5 0.6 constant_dynamic-update-slice_fusion.3
  105.1 0.6 constant_dynamic-update-slice_fusion.2
  105.8 0.6 constant_dynamic-update-slice_fusion.1
  106.4 0.6 constant_dynamic-update-slice_fusion
  107.0 0.6 fusion.41
  107.7 4.8 %all-to-all-start.1 = ((f32[16,128,128]{2,1,0:T(8,128)}), f32[16,128,128]{2,1,0:T(8,128)S(1)}, u32[]{:S(2)}, u32[]{:S(2)}) async-start(f32[16,128,128]{2,1,0:T(8,128)} %fusion.41), calls=%async_computation.1 | async-start | bytes 2097152 | tf_op jit(solution)/shard_map/all_to_all | solution.py:123
  112.4 0.5 multiply_reduce_fusion
  112.9 0.6 dynamic-slice_bitcast_fusion
  113.5 23.8 %all-to-all-done.1 = f32[16,128,128]{2,1,0:T(8,128)S(1)} async-done(((f32[16,128,128]{2,1,0:T(8,128)}), f32[16,128,128]{2,1,0:T(8,128)S(1)}, u32[]{:S(2)}, u32[]{:S(2)}) %all-to-all-start.1) | async-done | bytes 1048608 | tf_op jit(solution)/shard_map/all_to_all | solution.py:123
  137.4 1.0 copy.42
  (73 shorter events, 1.5 us)
Async XLA Ops:
  7.2 9.4 %copy-start = (s32[32]{0:T(128)S(1)}, s32[32]{0:T(128)}, u32[]{:S(2)}) copy-start(s32[32]{0:T(128)} %param.14) | copy-start | bytes 388
  7.2 2.9 %copy-start.2 = (f32[1,2048,128]{2,1,0:T(8,128)S(1)}, f32[1,2048,128]{2,1,0:T(8,128)}, u32[]{:S(2)}) copy-start(f32[1,2048,128]{2,1,0:T(8,128)} %param.11) | copy-start | bytes 3145732
  7.2 46.9 %all-reduce.2.cloned.1.call-start = ((), (), s32[]{:S(2)}) async-start(), calls=%async_computation.2 | async-start | bytes 524288 | tf_op jit(solution)/shard_map/psum | solution.py:87
  7.2 20.0 %collective-permute-start = (s32[4,128]{1,0:T(4,128)}, s32[4,128]{1,0:T(4,128)S(1)}, u32[]{:S(2)}, u32[]{:S(2)}) collective-permute-start(s32[4,128]{1,0:T(4,128)} %bitcast.274), channel_id=1, source_target_pairs={{0,1},{1,0},{2,3},{3,2},{4,5},{5,4},{6,7},{7,6},{8,9},{9,8},{10,11... | collective-permute-start | bytes 6152 | tf_op jit(solution)/shard_map/ppermute | solution.py:17
  8.5 8.0 %copy-start.5 = (s32[1,4,128]{2,1,0:T(4,128)S(1)}, s32[1,4,128]{2,1,0:T(4,128)}, u32[]{:S(2)}) copy-start(s32[1,4,128]{2,1,0:T(4,128)} %param.12) | copy-start | bytes 6148
  26.1 1.2 copy-start.6
  26.1 1.3 copy-start.4
  54.1 5.2 %copy-start.1 = (bf16[1024,128]{1,0:T(8,128)(2,1)S(1)}, bf16[1024,128]{1,0:T(8,128)(2,1)}, u32[]{:S(2)}) copy-start(bf16[1024,128]{1,0:T(8,128)(2,1)} %all-reduce.2.cloned.1.call-done) | copy-start | bytes 786436
  65.3 7.0 %copy-start.3 = (f32[128]{0:T(128)S(1)}, f32[128]{0:T(128)}, u32[]{:S(2)}) copy-start(f32[128]{0:T(128)} %param.16) | copy-start | bytes 1540
  65.3 31.9 %all-to-all-start = ((f32[16,128,128]{2,1,0:T(8,128)}), f32[16,128,128]{2,1,0:T(8,128)S(1)}, u32[]{:S(2)}, u32[]{:S(2)}) async-start(f32[16,128,128]{2,1,0:T(8,128)} %bitcast.58), calls=%async_computation | async-start | bytes 2097152 | tf_op jit(solution)/shard_map/all_to_all | solution.py:101
  107.7 29.7 %all-to-all-start.1 = ((f32[16,128,128]{2,1,0:T(8,128)}), f32[16,128,128]{2,1,0:T(8,128)S(1)}, u32[]{:S(2)}, u32[]{:S(2)}) async-start(f32[16,128,128]{2,1,0:T(8,128)} %fusion.41), calls=%async_computation.1 | async-start | bytes 2097152 | tf_op jit(solution)/shard_map/all_to_all | solution.py:123
Sparse Core Ops, SparseCore 0:
  27.3 26.7 all-reduce.1
